TPU v7x, 32 devices: a whole 2x2x4 slice. The times are simulated.
32 devices in a mesh: pair: 4 (over z), gen: 8 (over y, x, core).
Axes of the slice: x: 2, y: 2, z: 4, core: 2. Of those that a mesh axis runs over, the one named last changes fastest.
Arguments:
- tokens: bfloat16 [32768, 2048], P(('pair', 'gen')), may hold values from -6 to 6
- cotangent: bfloat16 [32768, 256], P(('pair', 'gen')), may hold values from -6 to 6
- block_pair: int32 [32, 1], replicated, may hold values from 0 to 15
- src_lang: int32 [16], replicated, may hold values from 0 to 95
- tgt_lang: int32 [16], replicated, may hold values from 0 to 95
- lang_embed: float32 [96, 512], P(None, 'pair'), may hold values from -5 to 5
- generator: bfloat16 [512, 524288], P('pair', 'gen'), may hold values from -0.005859375 to 0.005859375
Outputs:
- grad_tokens: bfloat16 [32768, 2048], P(('pair', 'gen'))
- grad_generator: bfloat16 [512, 524288], P('pair', 'gen')
- grad_embed: float32 [96, 512], P(None, 'pair')
Inputs may be any that keep to these rules, and one draw needn't show every extreme that they name: `block_pair`: every pair owns at least one block; block counts per pair are uneven.
All inputs are finite; a program needn't handle non-finite values.
Results may differ from a plain program's by a relative error of at most 0.007.
Values may be sent and summed in bfloat16 or wider, within the bound.
No kernel may reach another device: no remote copies, remote signals or barrier semaphores. Data moves between devices by JAX's collectives and lax.ppermute only.
A program may use at most 128 MiB of HBM per device.

v0:
```python
import jax
import jax.numpy as jnp
from jax import lax
from jax.sharding import PartitionSpec as P

BLK = 1024


def shards(tokens, cotangent, block_pair, src_lang, tgt_lang, lang_embed, generator):
    gen_count = lax.axis_size("gen")
    pair_count_axis = lax.axis_size("pair")
    blocks_here = tokens.shape[0] // BLK
    model_width = tokens.shape[1]
    adapter_rank = cotangent.shape[1]
    languages = lang_embed.shape[0]
    pair_count = src_lang.shape[0]
    chunk = generator.shape[1]
    quarter = chunk // pair_count_axis
    lang_ids = jnp.arange(languages, dtype=jnp.int32)
    hot_both = (src_lang[:, None] == lang_ids[None, :]).astype(jnp.float32) + (
        tgt_lang[:, None] == lang_ids[None, :]
    ).astype(jnp.float32)
    pair_embed = jnp.dot(hot_both, lang_embed, precision=lax.Precision.HIGHEST).astype(jnp.bfloat16)
    partial_value = jnp.dot(pair_embed, generator, preferred_element_type=jnp.float32)
    adapter_part = lax.psum_scatter(
        partial_value.astype(jnp.bfloat16), "pair", scatter_dimension=1, tiled=True
    )
    flat_pairs = block_pair[:, 0]
    outgoing = jnp.take(adapter_part, flat_pairs, axis=0)
    incoming = lax.all_to_all(outgoing, ("pair", "gen"), 0, 0, tiled=True)
    adapters = (
        incoming.reshape(pair_count_axis, gen_count, quarter)
        .transpose(1, 0, 2)
        .reshape(blocks_here, model_width, adapter_rank)
    )
    token_blocks = tokens.reshape(blocks_here, BLK, model_width)
    cot_blocks = cotangent.reshape(blocks_here, BLK, adapter_rank)
    hidden = jnp.einsum("btd,bdr->btr", token_blocks, adapters, preferred_element_type=jnp.float32)
    logistic = jax.nn.sigmoid(hidden)
    grad_hidden = (
        cot_blocks.astype(jnp.float32) * logistic * (1.0 + hidden * (1.0 - logistic))
    ).astype(jnp.bfloat16)
    grad_tokens = (
        jnp.einsum("btr,bdr->btd", grad_hidden, adapters, preferred_element_type=jnp.float32)
        .astype(jnp.bfloat16)
        .reshape(tokens.shape)
    )
    outer_grads = jnp.einsum(
        "btd,btr->bdr", token_blocks, grad_hidden, preferred_element_type=jnp.float32
    )
    by_owner = (
        outer_grads.reshape(gen_count, pair_count_axis, quarter)
        .transpose(1, 0, 2)
        .reshape(pair_count_axis * gen_count, quarter)
        .astype(jnp.bfloat16)
    )
    returned = lax.all_to_all(by_owner, ("pair", "gen"), 0, 0, tiled=True)
    pair_ids = jnp.arange(pair_count, dtype=jnp.int32)
    segment_hot = (pair_ids[:, None] == flat_pairs[None, :]).astype(jnp.float32)
    row_grad = jnp.dot(
        segment_hot, returned.astype(jnp.float32), precision=lax.Precision.HIGHEST
    ).astype(jnp.bfloat16)
    grad_rounded = lax.all_gather(row_grad, "pair", axis=1, tiled=True)
    grad_generator = jnp.einsum(
        "pe,pc->ec", pair_embed, grad_rounded, preferred_element_type=jnp.float32
    ).astype(jnp.bfloat16)
    partial_pair = jnp.einsum(
        "pc,ec->pe", grad_rounded, generator, preferred_element_type=jnp.float32
    )
    grad_pair = lax.psum(partial_pair, "gen")
    grad_embed = jnp.dot(hot_both.T, grad_pair, precision=lax.Precision.HIGHEST)
    return (grad_tokens, grad_generator, grad_embed)


def solution(mesh):
    placed = (
        P(("pair", "gen"), None),
        P(("pair", "gen"), None),
        P(),
        P(),
        P(),
        P(None, "pair"),
        P("pair", "gen"),
    )
    return jax.shard_map(
        shards,
        mesh=mesh,
        in_specs=placed,
        out_specs=(P(("pair", "gen"), None), P("pair", "gen"), P(None, "pair")),
        check_vma=False,
    )
```

profile of v0, /device:TPU:0, one launch (start us, length us, event | category | flops | bytes accessed | tf_op | source)
XLA Modules:
  0.0 235.5 jit_solution(6820055431846227179)
XLA Ops:
  8.0 0.9 convolution_convert_fusion.5
  8.9 9.4 %convolution_convert_fusion.1 = bf16[16,65536]{1,0:T(8,128)(2,1)} fusion(bf16[16,128]{1,0:T(8,128)(2,1)S(1)} %convolution_convert_fusion.5, bf16[128,65536]{1,0:T(8,128)(2,1)} %param.13), kind=kOutput, calls=%fused_computation.2 | convolution fusion | flops 269484032 | bytes 18878464 | tf_op jit(solution)/shard_map/dot_general | solution.py:24
  18.3 46.7 %reduce-scatter.2.cloned.1.call-done = bf16[16,16384]{1,0:T(8,128)(2,1)} async-done(((bf16[16,65536]{1,0:T(8,128)(2,1)}), bf16[16,16384]{1,0:T(8,128)(2,1)}) %reduce-scatter.2.cloned.1.call-update) | async-done | bytes 524304 | tf_op jit(solution)/shard_map/reduce_scatter | solution.py:25
  65.0 3.2 %gather_fusion = bf16[32,16384]{1,0:T(8,128)(2,1)S(1)} fusion(bf16[16,16384]{1,0:T(8,128)(2,1)} %reduce-scatter.2.cloned.1.call-done, s32[1024]{0:T(1024)S(1)} %pad_clamp_fusion), kind=kCustom, calls=%fused_computation | custom fusion | bytes 2097280 | tf_op jit(solution)/shard_map/jit(_take)/gather | solution.py:29
  68.9 1.4 reduce
  70.4 1.6 reshape.111
  72.0 3.9 %all-to-all-start = ((bf16[32,2,8192]{2,1,0:T(2,128)(2,1)}), bf16[32,2,8192]{2,1,0:T(2,128)(2,1)S(1)}, u32[]{:S(2)}, u32[]{:S(2)}) async-start(bf16[32,2,8192]{2,1,0:T(2,128)(2,1)} %reshape.111), calls=%async_computation.1 | async-start | bytes 2097152 | tf_op jit(solution)/shard_map/all_to_all | solution.py:30
  76.1 1.0 copy.21
  77.1 25.0 %all-to-all-done = bf16[32,2,8192]{2,1,0:T(2,128)(2,1)S(1)} async-done(((bf16[32,2,8192]{2,1,0:T(2,128)(2,1)}), bf16[32,2,8192]{2,1,0:T(2,128)(2,1)S(1)}, u32[]{:S(2)}, u32[]{:S(2)}) %all-to-all-start) | async-done | bytes 1048608 | tf_op jit(solution)/shard_map/all_to_all | solution.py:30
  102.1 1.0 reshape.112
  103.2 1.2 copy.35
  105.9 3.9 %convolution_bitcast_fusion = f32[1024,256]{0,1:T(8,128)S(1)} fusion(bf16[2048,256]{1,0:T(8,128)(2,1)S(1)} %reshape.102, bf16[1024,2048]{1,0:T(8,128)(2,1)} %param.7), kind=kOutput, calls=%fused_computation.7 | convolution fusion | flops 1073741824 | bytes 6291456 | tf_op jit(solution)/shard_map/btd,bdr->btr/dot_general | solution.py:38
  109.9 1.0 copy-done.10
  110.8 1.5 fusion
  114.3 1.4 reduce.1
  116.5 29.7 %all_to_all.15 = bf16[32,2,8192]{2,1,0:T(2,128)(2,1)S(1)} all-to-all(bf16[32,2,8192]{2,1,0:T(2,128)(2,1)S(1)} %reshape.113), channel_id=1, replica_groups=mesh['pair'=4,'gen'=8] {'pair','gen'}, dimensions={0} | all-to-all | bytes 2097152 | tf_op jit(solution)/shard_map/all_to_all | solution.py:57
  146.2 1.0 reshape.114
  147.3 2.0 convolution_convert_fusion.2
  149.3 5.3 %convolution_convert_fusion.3 = bf16[1024,2048]{1,0:T(8,128)(2,1)} fusion(bf16[2048,256]{1,0:T(8,128)(2,1)} %copy-done.3, f32[1024,256]{0,1:T(8,128)} %copy-done.10, bf16[1024,256]{0,1:T(8,128)(2,1)} %copy.21), kind=kOutput, calls=%fused_computation.4 | convolution fusion | flops 1078460416 | bytes 6815744 | tf_op jit(solution)/shard_map/btr,bdr->btd/dot_general | solution.py:44
  154.6 39.8 %all-gather.2.cloned.1.call-done = bf16[16,65536]{1,0:T(8,128)(2,1)} async-done(((bf16[16,16384]{1,0:T(8,128)(2,1)}), bf16[16,65536]{1,0:T(8,128)(2,1)}) %all-gather.2.cloned.1.call-update) | async-done | bytes 2097168 | tf_op jit(solution)/shard_map/all_gather | solution.py:63
  194.4 11.0 %fusion.16 = f32[16,128]{1,0:T(8,128)S(1)} fusion(bf16[16,65536]{1,0:T(8,128)(2,1)} %all-gather.2.cloned.1.call-done, bf16[128,65536]{1,0:T(8,128)(2,1)} %param.13), kind=kOutput, calls=%fused_computation.35 | convolution fusion | flops 268435456 | bytes 18882560 | tf_op jit(solution)/shard_map/pc,ec->pe/dot_general | solution.py:67
  205.4 13.8 %psum.7 = f32[16,128]{1,0:T(8,128)S(1)} all-reduce(f32[16,128]{1,0:T(8,128)S(1)} %fusion.16), channel_id=1, replica_groups=mesh['pair'=4,'gen'=8] {'gen'}, use_global_device_ids=true, to_apply=%region_1.2 | all-reduce | flops 2048 | bytes 16384 | tf_op jit(solution)/shard_map/psum | solution.py:70
  219.2 1.0 fusion.7
  220.2 8.5 %convolution_convert_fusion = bf16[128,65536]{1,0:T(8,128)(2,1)} fusion(bf16[16,128]{1,0:T(8,128)(2,1)S(1)} %convolution_convert_fusion.5, bf16[16,65536]{1,0:T(8,128)(2,1)S(1)} %copy-done.2), kind=kOutput, calls=%fused_computation.1 | convolution fusion | flops 276824064 | bytes 18878464 | tf_op jit(solution)/shard_map/pe,pc->ec/dot_general | solution.py:64
  (36 shorter events, 6.1 us)
Async XLA Ops:
  7.2 0.8 copy-start
  7.2 57.8 %reduce-scatter.2.cloned.1.call-start = ((), (), s32[]{:S(2)}) async-start(), calls=%async_computation.3 | async-start | bytes 2621440 | tf_op jit(solution)/shard_map/reduce_scatter | solution.py:25
  8.8 9.4 %copy-start.6 = (s32[32,1]{0,1:T(1,128)S(1)}, s32[32,1]{0,1:T(1,128)}, u32[]{:S(2)}) copy-start(s32[32,1]{0,1:T(1,128)} %param.9) | copy-start | bytes 388
  68.2 7.9 %copy-start.4 = (bf16[1024,256]{1,0:T(8,128)(2,1)S(1)}, bf16[1024,256]{1,0:T(8,128)(2,1)}, u32[]{:S(2)}) copy-start(bf16[1024,256]{1,0:T(8,128)(2,1)} %param.8) | copy-start | bytes 1572868
  72.0 30.1 %all-to-all-start = ((bf16[32,2,8192]{2,1,0:T(2,128)(2,1)}), bf16[32,2,8192]{2,1,0:T(2,128)(2,1)S(1)}, u32[]{:S(2)}, u32[]{:S(2)}) async-start(bf16[32,2,8192]{2,1,0:T(2,128)(2,1)} %reshape.111), calls=%async_computation.1 | async-start | bytes 2097152 | tf_op jit(solution)/shard_map/all_to_all | solution.py:30
  75.9 118.5 %all-gather.2.cloned.1.call-start = ((), (), s32[]{:S(2)}) async-start(), calls=%async_computation.4 | async-start | bytes 2621440 | tf_op jit(solution)/shard_map/all_gather | solution.py:63
  105.9 6.4 %copy-start.3 = (bf16[2048,256]{1,0:T(8,128)(2,1)}, bf16[2048,256]{1,0:T(8,128)(2,1)S(1)}, u32[]{:S(2)}) copy-start(bf16[2048,256]{1,0:T(8,128)(2,1)S(1)} %reshape.102) | copy-start | bytes 3145732
  105.9 4.9 %copy-start.5 = (bf16[1024,256]{0,1:T(8,128)(2,1)S(1)}, bf16[1024,256]{0,1:T(8,128)(2,1)}, u32[]{:S(2)}) copy-start(bf16[1024,256]{0,1:T(8,128)(2,1)} %copy.21) | copy-start | bytes 1572868
  105.9 4.9 %copy-start.7 = (bf16[1024,2048]{1,0:T(8,128)(2,1)S(1)}, bf16[1024,2048]{1,0:T(8,128)(2,1)}, u32[]{:S(2)}) copy-start(bf16[1024,2048]{1,0:T(8,128)(2,1)} %param.7) | copy-start | bytes 12582916
  109.8 1.0 copy-start.10
  154.6 64.6 %copy-start.8 = (s32[16]{0:T(128)S(1)}, s32[16]{0:T(128)}, u32[]{:S(2)}) copy-start(s32[16]{0:T(128)} %param.11) | copy-start | bytes 196
  154.6 64.6 %copy-start.9 = (s32[16]{0:T(128)S(1)}, s32[16]{0:T(128)}, u32[]{:S(2)}) copy-start(s32[16]{0:T(128)} %param.10) | copy-start | bytes 196
  194.4 25.8 %copy-start.2 = (bf16[16,65536]{1,0:T(8,128)(2,1)S(1)}, bf16[16,65536]{1,0:T(8,128)(2,1)}, u32[]{:S(2)}) copy-start(bf16[16,65536]{1,0:T(8,128)(2,1)} %all-gather.2.cloned.1.call-done) | copy-start | bytes 6291460
  220.2 8.5 %copy-start.1 = (f32[96,128]{1,0:T(8,128)S(1)}, f32[96,128]{1,0:T(8,128)}, u32[]{:S(2)}) copy-start(f32[96,128]{1,0:T(8,128)} %param.12) | copy-start | bytes 147460
Sparse Core Ops, SparseCore 0:
  18.4 46.5 reduce-scatter.1
  149.4 44.9 all-gather.1
where the time goes:
time: 236 us
  waiting for transfers between devices  111 us (47%)
  blocking collectives  43.5 us (18%)
  matrix products  43.4 us (18%)
  local copies, waits for them, and re-layouts  15.6 us (7%)
  between operations  14.3 us (6%)
  starting transfers between devices  4.17 us (2%)
  other arithmetic  3.07 us (1%)
    reduce_scatter x1, waiting for transfers between devices, shards(): lax.psum_scatter(partial_value.astype(jnp.bfloat16), 'pair', scatter_dime...  46.7 us
    all_gather x1, waiting for transfers between devices, shards(): grad_rounded = lax.all_gather(row_grad, 'pair', axis=1, tiled=True)  39.8 us
    all_to_all x1, blocking collectives, shards(): returned = lax.all_to_all(by_owner, ('pair', 'gen'), 0, 0, tiled=True)  29.7 us
    all_to_all x1, waiting for transfers between devices, shards(): incoming = lax.all_to_all(outgoing, ('pair', 'gen'), 0, 0, tiled=True)  25 us
    psum x1, blocking collectives, shards(): grad_pair = lax.psum(partial_pair, 'gen')  13.8 us
    dot_general x1, matrix products, shards(): jnp.einsum('pc,ec->pe', grad_rounded, generator, preferred_element_type=j...  11 us
    dot_general x1, matrix products, shards(): jnp.dot(pair_embed, generator, preferred_element_type=jnp.float32)  9.4 us
    dot_general x1, matrix products, shards(): jnp.einsum('pe,pc->ec', pair_embed, grad_rounded, preferred_element_type=...  8.52 us
  transfers between devices with their start and end apart: 3, of which 3 were waited for; matrix products, arithmetic and copies ran while one was open for 3% of the time, Pallas kernels for 0%

commit v1 on v0

--- a/solution.py
+++ b/solution.py
@@ -7,6 +7,13 @@
 
 
 def shards(tokens, cotangent, block_pair, src_lang, tgt_lang, lang_embed, generator):
+
+    def guide_trails(arr_in):
+        return jnp.concatenate(
+            jax.lax.all_to_all(jnp.stack(jax.lax.axis_size("pair") * [arr_in]), "pair", 0, 0),
+            axis=1,
+        )
+
     gen_count = lax.axis_size("gen")
     pair_count_axis = lax.axis_size("pair")
     blocks_here = tokens.shape[0] // BLK
@@ -60,7 +67,7 @@
     row_grad = jnp.dot(
         segment_hot, returned.astype(jnp.float32), precision=lax.Precision.HIGHEST
     ).astype(jnp.bfloat16)
-    grad_rounded = lax.all_gather(row_grad, "pair", axis=1, tiled=True)
+    grad_rounded = guide_trails(row_grad)
     grad_generator = jnp.einsum(
         "pe,pc->ec", pair_embed, grad_rounded, preferred_element_type=jnp.float32
     ).astype(jnp.bfloat16)

time: 236 us -> 243 us (1.030)
  local copies, waits for them, and re-layouts: 15.6 us -> 20.1 us
  matrix products: 43.4 us -> 39.5 us
  starting transfers between devices: 4.17 us -> 7.95 us
  waiting for transfers between devices: 111 us -> 114 us
    all_to_all x0 -> x1, waiting for transfers between devices: none -> 42.7 us  [guide_trails(): jax.lax.all_to_all(jnp.stack(jax.lax.axis_size('pair') * [arr_in]), 'pair...]
    all_gather x1 -> x0, waiting for transfers between devices: 39.8 us -> none  [shards(): grad_rounded = lax.all_gather(row_grad, 'pair', axis=1, tiled=True)]
    all_to_all x0 -> x1, starting transfers between devices: none -> 3.83 us  [guide_trails(): jax.lax.all_to_all(jnp.stack(jax.lax.axis_size('pair') * [arr_in]), 'pair...]
    dot_general x1, matrix products: 11 us -> 8.06 us  [shards(): jnp.einsum('pc,ec->pe', grad_rounded, generator, preferred_element_type=j...]
    unnamed x28 -> x30, local copies, waits for them, and re-layouts: 8.39 us -> 9.71 us
  transfers between devices with their start and end apart: 3 -> 3, of which waited for: 3 -> 3; matrix products, arithmetic and copies ran while one was open for 3% -> 2% of each run, Pallas kernels for 0% -> 0%
where the time goes in v1:
time: 243 us; the launch traced here: 242 us
  waiting for transfers between devices  114 us (47%)
  blocking collectives  42.8 us (18%)
  matrix products  39.5 us (16%)
  local copies, waits for them, and re-layouts  20.1 us (8%)
  between operations  14.3 us (6%)
  starting transfers between devices  7.95 us (3%)
  other arithmetic  3.07 us (1%)
    reduce_scatter x1, waiting for transfers between devices, shards(): lax.psum_scatter(partial_value.astype(jnp.bfloat16), 'pair', scatter_dime...  46.7 us
    all_to_all x1, waiting for transfers between devices, guide_trails(): jax.lax.all_to_all(jnp.stack(jax.lax.axis_size('pair') * [arr_in]), 'pair...  42.7 us
    all_to_all x1, blocking collectives, shards(): returned = lax.all_to_all(by_owner, ('pair', 'gen'), 0, 0, tiled=True)  29.7 us
    all_to_all x1, waiting for transfers between devices, shards(): incoming = lax.all_to_all(outgoing, ('pair', 'gen'), 0, 0, tiled=True)  25 us
    psum x1, blocking collectives, shards(): grad_pair = lax.psum(partial_pair, 'gen')  13.2 us
    unnamed x30, local copies, waits for them, and re-layouts  9.71 us
    dot_general x1, matrix products, shards(): jnp.dot(pair_embed, generator, preferred_element_type=jnp.float32)  9.4 us
    dot_general x1, matrix products, shards(): jnp.einsum('pe,pc->ec', pair_embed, grad_rounded, preferred_element_type=...  8.55 us
  transfers between devices with their start and end apart: 3, of which 3 were waited for; matrix products, arithmetic and copies ran while one was open for 2% of the time, Pallas kernels for 0%

profile of v1, /device:TPU:0, one launch (start us, length us, event | category | flops | bytes accessed | tf_op | source)
XLA Modules:
  0.0 242.2 jit_solution(1088679371082069394)
XLA Ops:
  8.9 9.4 %convolution_convert_fusion.1 = bf16[16,65536]{1,0:T(8,128)(2,1)} fusion(bf16[16,128]{1,0:T(8,128)(2,1)S(1)} %convolution_convert_fusion.5, bf16[128,65536]{1,0:T(8,128)(2,1)} %param.13), kind=kOutput, calls=%fused_computation.2 | convolution fusion | flops 269484032 | bytes 18878464 | tf_op jit(solution)/shard_map/dot_general | solution.py:31
  18.3 46.7 %reduce-scatter.2.cloned.1.call-done = bf16[16,16384]{1,0:T(8,128)(2,1)} async-done(((bf16[16,65536]{1,0:T(8,128)(2,1)}), bf16[16,16384]{1,0:T(8,128)(2,1)}) %reduce-scatter.2.cloned.1.call-update) | async-done | bytes 524304 | tf_op jit(solution)/shard_map/reduce_scatter | solution.py:32
  65.0 3.2 %gather_fusion = bf16[32,16384]{1,0:T(8,128)(2,1)S(1)} fusion(bf16[16,16384]{1,0:T(8,128)(2,1)} %reduce-scatter.2.cloned.1.call-done, s32[1024]{0:T(1024)S(1)} %pad_clamp_fusion), kind=kCustom, calls=%fused_computation | custom fusion | bytes 2097280 | tf_op jit(solution)/shard_map/jit(_take)/gather | solution.py:36
  68.9 1.4 reduce
  70.4 1.6 reshape.121
  72.0 4.1 %all-to-all-start = ((bf16[32,2,8192]{2,1,0:T(2,128)(2,1)}), bf16[32,2,8192]{2,1,0:T(2,128)(2,1)S(1)}, u32[]{:S(2)}, u32[]{:S(2)}) async-start(bf16[32,2,8192]{2,1,0:T(2,128)(2,1)} %reshape.121), calls=%async_computation.1 | async-start | bytes 2097152 | tf_op jit(solution)/shard_map/all_to_all | solution.py:37
  77.1 25.0 %all-to-all-done = bf16[32,2,8192]{2,1,0:T(2,128)(2,1)S(1)} async-done(((bf16[32,2,8192]{2,1,0:T(2,128)(2,1)}), bf16[32,2,8192]{2,1,0:T(2,128)(2,1)S(1)}, u32[]{:S(2)}, u32[]{:S(2)}) %all-to-all-start) | async-done | bytes 1048608 | tf_op jit(solution)/shard_map/all_to_all | solution.py:37
  102.1 1.0 reshape.122
  103.2 1.2 copy.38
  105.9 3.9 %convolution_bitcast_fusion = f32[1024,256]{0,1:T(8,128)S(1)} fusion(bf16[2048,256]{1,0:T(8,128)(2,1)S(1)} %reshape.110, bf16[1024,2048]{1,0:T(8,128)(2,1)} %param.7), kind=kOutput, calls=%fused_computation.7 | convolution fusion | flops 1073741824 | bytes 6291456 | tf_op jit(solution)/shard_map/btd,bdr->btr/dot_general | solution.py:45
  110.8 1.5 fusion
  114.3 1.4 reduce.1
  116.6 29.7 %all_to_all.20 = bf16[32,2,8192]{2,1,0:T(2,128)(2,1)S(1)} all-to-all(bf16[32,2,8192]{2,1,0:T(2,128)(2,1)S(1)} %reshape.123), channel_id=1, replica_groups=mesh['pair'=4,'gen'=8] {'pair','gen'}, dimensions={0} | all-to-all | bytes 2097152 | tf_op jit(solution)/shard_map/all_to_all | solution.py:64
  146.2 1.0 reshape.124
  147.3 1.2 convolution_convert_fusion.2
  148.5 1.5 stack.2
  150.0 3.8 %all-to-all-start.2 = ((bf16[4,16,16384]{2,1,0:T(8,128)(2,1)}), bf16[4,16,16384]{2,1,0:T(8,128)(2,1)S(1)}, u32[]{:S(2)}, u32[]{:S(2)}) async-start(bf16[4,16,16384]{2,1,0:T(8,128)(2,1)} %stack.2), calls=%async_computation.3 | async-start | bytes 4194304 | tf_op jit(solution)/shard_map/all_to_all | solution.py:13
  153.8 5.0 %convolution_convert_fusion.3 = bf16[1024,2048]{1,0:T(8,128)(2,1)} fusion(bf16[2048,256]{1,0:T(8,128)(2,1)S(1)} %copy-done.4, f32[1024,256]{0,1:T(8,128)} %copy-done.11, bf16[1024,256]{0,1:T(8,128)(2,1)} %copy.22), kind=kOutput, calls=%fused_computation.4 | convolution fusion | flops 1078460416 | bytes 6815744 | tf_op jit(solution)/shard_map/btr,bdr->btd/dot_general | solution.py:51
  158.8 42.7 %all-to-all-done.2 = bf16[4,16,16384]{2,1,0:T(8,128)(2,1)S(1)} async-done(((bf16[4,16,16384]{2,1,0:T(8,128)(2,1)}), bf16[4,16,16384]{2,1,0:T(8,128)(2,1)S(1)}, u32[]{:S(2)}, u32[]{:S(2)}) %all-to-all-start.2) | async-done | bytes 2097184 | tf_op jit(solution)/shard_map/all_to_all | solution.py:13
  201.5 1.3 copy-done.2
  202.8 1.7 copy.31
  204.6 8.5 %convolution_convert_fusion = bf16[128,65536]{1,0:T(8,128)(2,1)} fusion(bf16[16,128]{1,0:T(8,128)(2,1)S(1)} %convolution_convert_fusion.5, bf16[16,65536]{1,0:T(8,128)(2,1)S(1)} %bitcast.38), kind=kOutput, calls=%fused_computation.1 | convolution fusion | flops 276824064 | bytes 18878464 | tf_op jit(solution)/shard_map/pe,pc->ec/dot_general | solution.py:71
  213.1 8.1 %fusion.16 = f32[16,128]{1,0:T(8,128)S(1)} fusion(bf16[16,65536]{1,0:T(8,128)(2,1)S(1)} %bitcast.39, bf16[128,65536]{1,0:T(8,128)(2,1)} %param.13), kind=kOutput, calls=%fused_computation.35 | convolution fusion | flops 268435456 | bytes 18882560 | tf_op jit(solution)/shard_map/pc,ec->pe/dot_general | solution.py:74
  221.2 13.2 %psum.7 = f32[16,128]{1,0:T(8,128)S(1)} all-reduce(f32[16,128]{1,0:T(8,128)S(1)} %fusion.16), channel_id=1, replica_groups=mesh['pair'=4,'gen'=8] {'gen'}, use_global_device_ids=true, to_apply=%region_1.2 | all-reduce | flops 2048 | bytes 16384 | tf_op jit(solution)/shard_map/psum | solution.py:77
  (39 shorter events, 9.7 us)
Async XLA Ops:
  7.2 0.8 copy-start
  7.2 57.8 %reduce-scatter.2.cloned.1.call-start = ((), (), s32[]{:S(2)}) async-start(), calls=%async_computation.4 | async-start | bytes 2621440 | tf_op jit(solution)/shard_map/reduce_scatter | solution.py:32
  8.8 9.4 %copy-start.7 = (s32[32,1]{0,1:T(1,128)S(1)}, s32[32,1]{0,1:T(1,128)}, u32[]{:S(2)}) copy-start(s32[32,1]{0,1:T(1,128)} %param.9) | copy-start | bytes 388
  68.2 7.8 %copy-start.5 = (bf16[1024,256]{1,0:T(8,128)(2,1)S(1)}, bf16[1024,256]{1,0:T(8,128)(2,1)}, u32[]{:S(2)}) copy-start(bf16[1024,256]{1,0:T(8,128)(2,1)} %param.8) | copy-start | bytes 1572868
  72.0 30.2 %all-to-all-start = ((bf16[32,2,8192]{2,1,0:T(2,128)(2,1)}), bf16[32,2,8192]{2,1,0:T(2,128)(2,1)S(1)}, u32[]{:S(2)}, u32[]{:S(2)}) async-start(bf16[32,2,8192]{2,1,0:T(2,128)(2,1)} %reshape.121), calls=%async_computation.1 | async-start | bytes 2097152 | tf_op jit(solution)/shard_map/all_to_all | solution.py:37
  105.9 6.5 %copy-start.3 = (bf16[2048,256]{1,0:T(8,128)(2,1)}, bf16[2048,256]{1,0:T(8,128)(2,1)S(1)}, u32[]{:S(2)}) copy-start(bf16[2048,256]{1,0:T(8,128)(2,1)S(1)} %reshape.110) | copy-start | bytes 3145732
  105.9 4.9 %copy-start.6 = (bf16[1024,256]{0,1:T(8,128)(2,1)S(1)}, bf16[1024,256]{0,1:T(8,128)(2,1)}, u32[]{:S(2)}) copy-start(bf16[1024,256]{0,1:T(8,128)(2,1)} %copy.22) | copy-start | bytes 1572868
  105.9 4.9 %copy-start.8 = (bf16[1024,2048]{1,0:T(8,128)(2,1)S(1)}, bf16[1024,2048]{1,0:T(8,128)(2,1)}, u32[]{:S(2)}) copy-start(bf16[1024,2048]{1,0:T(8,128)(2,1)} %param.7) | copy-start | bytes 12582916
  109.8 1.0 copy-start.11
  147.3 6.5 %copy-start.4 = (bf16[2048,256]{1,0:T(8,128)(2,1)S(1)}, bf16[2048,256]{1,0:T(8,128)(2,1)}, u32[]{:S(2)}) copy-start(bf16[2048,256]{1,0:T(8,128)(2,1)} %copy-done.3) | copy-start | bytes 3145732
  150.0 51.6 %all-to-all-start.2 = ((bf16[4,16,16384]{2,1,0:T(8,128)(2,1)}), bf16[4,16,16384]{2,1,0:T(8,128)(2,1)S(1)}, u32[]{:S(2)}, u32[]{:S(2)}) async-start(bf16[4,16,16384]{2,1,0:T(8,128)(2,1)} %stack.2), calls=%async_computation.3 | async-start | bytes 4194304 | tf_op jit(solution)/shard_map/all_to_all | solution.py:13
  201.5 1.3 copy-start.2
  213.1 21.2 %copy-start.9 = (s32[16]{0:T(128)S(1)}, s32[16]{0:T(128)}, u32[]{:S(2)}) copy-start(s32[16]{0:T(128)} %param.11) | copy-start | bytes 196
  213.1 21.3 %copy-start.10 = (s32[16]{0:T(128)S(1)}, s32[16]{0:T(128)}, u32[]{:S(2)}) copy-start(s32[16]{0:T(128)} %param.10) | copy-start | bytes 196
  213.1 22.2 %copy-start.1 = (f32[96,128]{1,0:T(8,128)S(1)}, f32[96,128]{1,0:T(8,128)}, u32[]{:S(2)}) copy-start(f32[96,128]{1,0:T(8,128)} %param.12) | copy-start | bytes 147460
Sparse Core Ops, SparseCore 0:
  18.4 46.5 reduce-scatter.1
